TPU v7x, 256 devices: a whole 4x4x8 slice. The times are simulated.
256 devices in a mesh: island: 4 (over x_lo, core), fsdp: 64 (over x_hi, z, y).
Axes of the slice: x: 4 (x_hi: 2, x_lo: 2; x = x_hi * 2 + x_lo), y: 4, z: 8, core: 2. Of those that a mesh axis runs over, the one named last changes fastest.
Arguments:
- acts: bfloat16 [65536, 8192], P(('island', 'fsdp')), may hold values from -24 to 24
- cotangent: bfloat16 [65536, 512], P(('island', 'fsdp')), may hold values from -6 to 6
- global_params: float32 [8192, 512], P('fsdp'), may hold values from -0.12 to 0.12
- momentum: float32 [8192, 512], P('fsdp'), may hold values from -0.18 to 0.18
- island_drift: float32 [4, 8192, 512], P('island', 'fsdp'), may hold values from -0.12 to 0.12
- moment1: float32 [4, 8192, 512], P('island', 'fsdp'), may hold values from -6 to 6
- moment2: float32 [4, 8192, 512], P('island', 'fsdp'), may hold values from 0.05 to 1
Outputs:
- keys: bfloat16 [65536, 512], P(('island', 'fsdp'))
- new_global: float32 [8192, 512], P('fsdp')
- new_momentum: float32 [8192, 512], P('fsdp')
- moment1_out: float32 [4, 8192, 512], P('island', 'fsdp')
- moment2_out: float32 [4, 8192, 512], P('island', 'fsdp')
All inputs are finite; a program needn't handle non-finite values.
Results may differ from a plain program's by a relative error of at most 0.0049.
Values may be sent and summed in bfloat16 or wider, within the bound.
No kernel may reach another device: no remote copies, remote signals or barrier semaphores. Data moves between devices by JAX's collectives and lax.ppermute only.
A program may use at most 128 MiB of HBM per device.

v0:
```python
import jax
import jax.numpy as jnp
from jax import lax
from jax.sharding import Mesh, PartitionSpec as P

D = 8192
FS = ("xh", "z", "y")
beta_one = 0.9
beta_two = 0.95
epsilon = 1e-08
inner_rate = 0.05
decay_rate = 0.1
outer_rate = 0.7
nesterov = 0.9


def per_device(acts, cotangent, global_params, momentum, island_drift, moment1, moment2):
    fsdp_count = lax.axis_size(FS)
    island_count = lax.axis_size("island")
    scale = (acts.shape[0] * fsdp_count) ** (-0.5)
    xh_n, z_n, y_n = (lax.axis_size(a) for a in ("xh", "z", "y"))
    tokens = acts.shape[0]
    acts_perm = (
        acts.reshape(tokens, xh_n, z_n, D // (xh_n * z_n)).transpose(0, 2, 1, 3).reshape(tokens, D)
    )
    partial = lax.dot_general(
        acts_perm, cotangent, (((0,), (0,)), ((), ())), preferred_element_type=jnp.float32
    )
    grad = lax.psum_scatter(partial, "z", scatter_dimension=0, tiled=True)
    grad = lax.psum_scatter(grad, "xh", scatter_dimension=0, tiled=True)
    grad = lax.psum_scatter(grad, "y", scatter_dimension=0, tiled=True)
    grad = grad * scale
    drift = island_drift[0]
    first = beta_one * moment1[0] + (1.0 - beta_one) * grad
    second = beta_two * moment2[0] + (1.0 - beta_two) * grad * grad
    step = first / (jnp.sqrt(second) + epsilon) + decay_rate * (global_params - drift)
    pseudo = drift + inner_rate * step
    pair_core = [(i, i ^ 1) for i in range(island_count)]
    pair_chip = [(i, i ^ 2) for i in range(island_count)]
    summed = pseudo + lax.ppermute(pseudo, "island", pair_core)
    summed = summed + lax.ppermute(summed, "island", pair_chip)
    mean = summed / island_count
    new_momentum = nesterov * momentum + mean
    new_global = global_params - outer_rate * (mean + nesterov * new_momentum)
    weights = new_global.astype(jnp.bfloat16)
    core = lax.axis_index("island") % 2
    half = weights.shape[1] // 2
    own = lax.dynamic_slice_in_dim(weights, core * half, half, axis=1)
    own_full = lax.all_gather(own, FS, axis=0, tiled=True)
    other_full = lax.ppermute(own_full, "island", pair_core)
    keys_own = jnp.dot(acts, own_full, preferred_element_type=jnp.float32)
    keys_other = jnp.dot(acts, other_full, preferred_element_type=jnp.float32)
    keys_own = (keys_own * D ** (-0.5)).astype(jnp.bfloat16)
    keys_other = (keys_other * D ** (-0.5)).astype(jnp.bfloat16)
    is_first = core == 0
    keys = jnp.concatenate(
        [jnp.where(is_first, keys_own, keys_other), jnp.where(is_first, keys_other, keys_own)],
        axis=1,
    )
    return (keys, new_global, new_momentum, first[None], second[None])


def solution(mesh):
    fsdp_n = mesh.shape["fsdp"]
    mesh = Mesh(mesh.devices.reshape(mesh.shape["island"], 2, 8, fsdp_n // 16), ("island",) + FS)
    return jax.shard_map(
        per_device,
        mesh=mesh,
        in_specs=(
            P(("island", *FS), None),
            P(("island", *FS), None),
            P(FS, None),
            P(FS, None),
            P("island", FS, None),
            P("island", FS, None),
            P("island", FS, None),
        ),
        out_specs=(
            P(("island", *FS), None),
            P(FS, None),
            P(FS, None),
            P("island", FS, None),
            P("island", FS, None),
        ),
        check_vma=False,
    )
```

profile of v0, /device:TPU:1, one launch (start us, length us, event | category | flops | bytes accessed | tf_op | source)
XLA Modules:
  0.0 432.0 jit_solution(1409496534043252752)
XLA Ops:
  7.2 0.0 reduce-scatter.4.cloned.1.call-start
  7.2 6.4 %copy.14 = bf16[256,8192]{0,1:T(8,128)(2,1)} copy(bf16[256,8192]{1,0:T(8,128)(2,1)} %param.7) | data formatting | bytes 8388608 | tf_op args[0]
  13.6 2.5 copy.15
  16.1 8.1 %fusion.7 = f32[8192,512]{1,0:T(8,128)} fusion(bf16[256,8192]{0,1:T(8,128)(2,1)S(1)} %bitcast.42, bf16[256,512]{1,0:T(8,128)(2,1)S(1)} %copy-done), kind=kOutput, calls=%fused_computation.20 | convolution fusion | flops 2147483648 | bytes 21233664 | tf_op jit(solution)/shard_map/dot_general | solution.py:26
  24.2 0.0 reduce-scatter.4.cloned.1.call-update
  24.3 0.0 reduce-scatter.6.cloned.1.call-start
  24.3 177.4 %reduce-scatter.4.cloned.1.call-done = f32[1024,512]{1,0:T(8,128)} async-done(((f32[8192,512]{1,0:T(8,128)}), f32[1024,512]{1,0:T(8,128)}) %reduce-scatter.4.cloned.1.call-update) | async-done | bytes 2097168 | tf_op jit(solution)/shard_map/reduce_scatter | solution.py:29
  201.7 0.0 reduce-scatter.8.cloned.1.call-start
  201.8 39.5 %reduce-scatter.6.cloned.1.call-done = f32[512,512]{1,0:T(8,128)} async-done(((f32[1024,512]{1,0:T(8,128)}), f32[512,512]{1,0:T(8,128)}) %reduce-scatter.6.cloned.1.call-update) | async-done | bytes 1048592 | tf_op jit(solution)/shard_map/reduce_scatter | solution.py:30
  241.2 0.0 all-gather.2.cloned.1.call-start
  241.3 27.0 %reduce-scatter.8.cloned.1.call-done = f32[128,512]{1,0:T(8,128)} async-done(((f32[512,512]{1,0:T(8,128)}), f32[128,512]{1,0:T(8,128)}) %reduce-scatter.8.cloned.1.call-update) | async-done | bytes 262160 | tf_op jit(solution)/shard_map/reduce_scatter | solution.py:31
  268.3 1.9 fusion.6
  270.2 2.2 collective-permute-start
  272.4 1.2 collective-permute-done
  273.6 1.3 collective-permute-start.1
  274.9 6.3 %collective-permute-done.1 = f32[128,512]{1,0:T(8,128)S(1)} collective-permute-done((f32[128,512]{1,0:T(8,128)S(1)}, f32[128,512]{1,0:T(8,128)S(1)}, u32[]{:S(2)}, u32[]{:S(2)}) %collective-permute-start.1) | collective-permute-done | bytes 262176 | tf_op jit(solution)/shard_map/ppermute | solution.py:41
  281.2 0.8 multiply_subtract_fusion
  282.0 0.7 dynamic-slice_convert_fusion
  282.8 124.4 %all-gather.2.cloned.1.call-done = bf16[8192,256]{1,0:T(8,128)(2,1)} async-done(((bf16[128,256]{1,0:T(8,128)(2,1)}), bf16[8192,256]{1,0:T(8,128)(2,1)}) %all-gather.2.cloned.1.call-update) | async-done | bytes 4194320 | tf_op jit(solution)/shard_map/all_gather | solution.py:49
  407.1 4.2 collective-permute-start.2
  411.4 7.1 %collective-permute-done.2 = bf16[8192,256]{1,0:T(8,128)(2,1)} collective-permute-done((bf16[8192,256]{1,0:T(8,128)(2,1)}, bf16[8192,256]{1,0:T(8,128)(2,1)}, u32[]{:S(2)}, u32[]{:S(2)}) %collective-permute-start.2) | collective-permute-done | bytes 4194336 | tf_op jit(solution)/shard_map/ppermute | solution.py:50
  418.5 4.8 %fusion.1 = bf16[256,256]{1,0:T(8,128)(2,1)S(1)} fusion(bf16[8192,256]{1,0:T(8,128)(2,1)} %collective-permute-done.2, bf16[256,8192]{1,0:T(8,128)(2,1)} %param.7), kind=kOutput, calls=%fused_computation.3 | convolution fusion | flops 1073872896 | bytes 8519680 | tf_op jit(solution)/shard_map/dot_general | solution.py:52
  423.3 1.3 select_bitcast_fusion.1
  424.6 0.8 copy.16
  (23 shorter events, 0.2 us)
Async XLA Ops:
  7.2 8.9 %copy-start = (bf16[256,512]{1,0:T(8,128)(2,1)S(1)}, bf16[256,512]{1,0:T(8,128)(2,1)}, u32[]{:S(2)}) copy-start(bf16[256,512]{1,0:T(8,128)(2,1)} %param.8) | copy-start | bytes 786436
  7.2 194.5 %reduce-scatter.4.cloned.1.call-start = ((), (), s32[]{:S(2)}) async-start(), calls=%async_computation.3 | async-start | bytes 18874368 | tf_op jit(solution)/shard_map/reduce_scatter | solution.py:29
  24.2 244.1 %copy-start.2 = (f32[128,512]{1,0:T(8,128)S(1)}, f32[128,512]{1,0:T(8,128)}, u32[]{:S(2)}) copy-start(f32[128,512]{1,0:T(8,128)} %param.9) | copy-start | bytes 786436
  24.2 244.1 %copy-start.5 = (f32[1,128,512]{2,1,0:T(8,128)S(1)}, f32[1,128,512]{2,1,0:T(8,128)}, u32[]{:S(2)}) copy-start(f32[1,128,512]{2,1,0:T(8,128)} %param.13) | copy-start | bytes 786436
  24.2 244.1 %copy-start.6 = (f32[1,128,512]{2,1,0:T(8,128)S(1)}, f32[1,128,512]{2,1,0:T(8,128)}, u32[]{:S(2)}) copy-start(f32[1,128,512]{2,1,0:T(8,128)} %param.12) | copy-start | bytes 786436
  24.2 244.1 %copy-start.7 = (f32[1,128,512]{2,1,0:T(8,128)S(1)}, f32[1,128,512]{2,1,0:T(8,128)}, u32[]{:S(2)}) copy-start(f32[1,128,512]{2,1,0:T(8,128)} %param.11) | copy-start | bytes 786436
  24.2 257.0 %copy-start.4 = (f32[128,512]{1,0:T(8,128)S(1)}, f32[128,512]{1,0:T(8,128)}, u32[]{:S(2)}) copy-start(f32[128,512]{1,0:T(8,128)} %param.10) | copy-start | bytes 786436
  24.3 217.0 %reduce-scatter.6.cloned.1.call-start = ((), (), s32[]{:S(2)}) async-start(), calls=%async_computation.4 | async-start | bytes 3145728 | tf_op jit(solution)/shard_map/reduce_scatter | solution.py:30
  201.7 66.6 %reduce-scatter.8.cloned.1.call-start = ((), (), s32[]{:S(2)}) async-start(), calls=%async_computation.5 | async-start | bytes 1310720 | tf_op jit(solution)/shard_map/reduce_scatter | solution.py:31
  241.2 165.9 %all-gather.2.cloned.1.call-start = ((), (), s32[]{:S(2)}) async-start(), calls=%async_computation.6 | async-start | bytes 4259840 | tf_op jit(solution)/shard_map/all_gather | solution.py:49
  270.2 3.4 collective-permute-start
  273.6 7.6 %collective-permute-start.1 = (f32[128,512]{1,0:T(8,128)S(1)}, f32[128,512]{1,0:T(8,128)S(1)}, u32[]{:S(2)}, u32[]{:S(2)}) collective-permute-start(f32[128,512]{1,0:T(8,128)S(1)} %add.50), channel_id=1, source_target_pairs={{0,128},{64,192},{128,0},{192,64},{1,129},{65,193},{129,1},{193,65... | collective-permute-start | bytes 786440 | tf_op jit(solution)/shard_map/ppermute | solution.py:41
  282.0 141.2 %copy-start.3 = (f32[128,512]{1,0:T(8,128)}, f32[128,512]{1,0:T(8,128)S(1)}, u32[]{:S(2)}) copy-start(f32[128,512]{1,0:T(8,128)S(1)} %get-tuple-element.20) | copy-start | bytes 786436
  407.1 11.4 %collective-permute-start.2 = (bf16[8192,256]{1,0:T(8,128)(2,1)}, bf16[8192,256]{1,0:T(8,128)(2,1)}, u32[]{:S(2)}, u32[]{:S(2)}) collective-permute-start(bf16[8192,256]{1,0:T(8,128)(2,1)} %all-gather.2.cloned.1.call-done), channel_id=1, source_target_pairs={{0,64},{64,0},{128,192},{192,128},{1,65},{65,1},{129,193},{193,129... | collective-permute-start | bytes 12582920 | tf_op jit(solution)/shard_map/ppermute | solution.py:50
  411.3 11.9 %copy-start.1 = (bf16[256,8192]{1,0:T(8,128)(2,1)S(1)}, bf16[256,8192]{1,0:T(8,128)(2,1)}, u32[]{:S(2)}) copy-start(bf16[256,8192]{1,0:T(8,128)(2,1)} %param.7) | copy-start | bytes 12582916
  411.3 11.9 %copy-start.8 = (bf16[8192,256]{1,0:T(8,128)(2,1)S(1)}, bf16[8192,256]{1,0:T(8,128)(2,1)}, u32[]{:S(2)}) copy-start(bf16[8192,256]{1,0:T(8,128)(2,1)} %all-gather.2.cloned.1.call-done) | copy-start | bytes 12582916
Sparse Core Ops, SparseCore 0:
  24.4 177.2 reduce-scatter.3
  204.2 36.9 reduce-scatter.5
  243.8 24.4 reduce-scatter.7
  282.9 124.1 all-gather.1
where the time goes:
time: 432 us
  waiting for transfers between devices  383 us (89%)
  matrix products  14.2 us (3%)
  between operations  13.9 us (3%)
  local copies, waits for them, and re-layouts  10.4 us (2%)
  starting transfers between devices  7.87 us (2%)
    reduce_scatter x1, waiting for transfers between devices, per_device(): grad = lax.psum_scatter(partial, 'z', scatter_dimension=0, tiled=True)  177 us
    all_gather x1, waiting for transfers between devices, per_device(): own_full = lax.all_gather(own, FS, axis=0, tiled=True)  124 us
    reduce_scatter x1, waiting for transfers between devices, per_device(): grad = lax.psum_scatter(grad, 'xh', scatter_dimension=0, tiled=True)  39.5 us
    reduce_scatter x1, waiting for transfers between devices, per_device(): grad = lax.psum_scatter(grad, 'y', scatter_dimension=0, tiled=True)  27 us
  transfers between devices with their start and end apart: 7, of which 7 were waited for; matrix products, arithmetic and copies ran while one was open for 0% of the time, Pallas kernels for 0%

commit v1 on v0

--- a/solution.py
+++ b/solution.py
@@ -46,7 +46,9 @@
     core = lax.axis_index("island") % 2
     half = weights.shape[1] // 2
     own = lax.dynamic_slice_in_dim(weights, core * half, half, axis=1)
-    own_full = lax.all_gather(own, FS, axis=0, tiled=True)
+    own_full = jnp.concatenate(
+        lax.all_to_all(jnp.stack([own] * lax.axis_size(FS)), FS, 0, 0), axis=0
+    )
     other_full = lax.ppermute(own_full, "island", pair_core)
     keys_own = jnp.dot(acts, own_full, preferred_element_type=jnp.float32)
     keys_other = jnp.dot(acts, other_full, preferred_element_type=jnp.float32)

time: 432 us -> 410 us (0.949)
  waiting for transfers between devices: 383 us -> 254 us
  blocking collectives: 0 us -> 105 us
    all_gather x1 -> x0, waiting for transfers between devices: 124 us -> none  [per_device(): own_full = lax.all_gather(own, FS, axis=0, tiled=True)]
    all_to_all x0 -> x1, blocking collectives: none -> 105 us  [per_device(): lax.all_to_all(jnp.stack([own] * lax.axis_size(FS)), FS, 0, 0)]
    ppermute x1, waiting for transfers between devices: 7.12 us -> 2.22 us  [per_device(): other_full = lax.ppermute(own_full, 'island', pair_core)]
  transfers between devices with their start and end apart: 7 -> 6, of which waited for: 7 -> 6; matrix products, arithmetic and copies ran while one was open for 0% -> 1% of each run, Pallas kernels for 0% -> 0%
where the time goes in v1:
time: 410 us; the launch traced here: 409 us
  waiting for transfers between devices  254 us (62%)
  blocking collectives  105 us (26%)
  matrix products  16.5 us (4%)
  between operations  13.8 us (3%)
  local copies, waits for them, and re-layouts  10.3 us (3%)
  starting transfers between devices  7.4 us (2%)
    reduce_scatter x1, waiting for transfers between devices, per_device(): grad = lax.psum_scatter(partial, 'z', scatter_dimension=0, tiled=True)  177 us
    all_to_all x1, blocking collectives, per_device(): lax.all_to_all(jnp.stack([own] * lax.axis_size(FS)), FS, 0, 0)  105 us
    reduce_scatter x1, waiting for transfers between devices, per_device(): grad = lax.psum_scatter(grad, 'xh', scatter_dimension=0, tiled=True)  39.5 us
    reduce_scatter x1, waiting for transfers between devices, per_device(): grad = lax.psum_scatter(grad, 'y', scatter_dimension=0, tiled=True)  27 us
  transfers between devices with their start and end apart: 6, of which 6 were waited for; matrix products, arithmetic and copies ran while one was open for 1% of the time, Pallas kernels for 0%

profile of v1, /device:TPU:1, one launch (start us, length us, event | category | flops | bytes accessed | tf_op | source)
XLA Modules:
  0.0 409.1 jit_solution(15761667640762347669)
XLA Ops:
  7.2 0.0 reduce-scatter.4.cloned.1.call-start
  7.2 6.4 %copy.14 = bf16[256,8192]{0,1:T(8,128)(2,1)} copy(bf16[256,8192]{1,0:T(8,128)(2,1)} %param.7) | data formatting | bytes 8388608 | tf_op args[0]
  13.6 2.5 copy.15
  16.1 8.1 %fusion.7 = f32[8192,512]{1,0:T(8,128)} fusion(bf16[256,8192]{0,1:T(8,128)(2,1)S(1)} %bitcast.43, bf16[256,512]{1,0:T(8,128)(2,1)S(1)} %copy-done), kind=kOutput, calls=%fused_computation.20 | convolution fusion | flops 2147483648 | bytes 21233664 | tf_op jit(solution)/shard_map/dot_general | solution.py:26
  24.2 0.0 reduce-scatter.4.cloned.1.call-update
  24.2 0.0 reduce-scatter.6.cloned.1.call-start
  24.3 177.4 %reduce-scatter.4.cloned.1.call-done = f32[1024,512]{1,0:T(8,128)} async-done(((f32[8192,512]{1,0:T(8,128)}), f32[1024,512]{1,0:T(8,128)}) %reduce-scatter.4.cloned.1.call-update) | async-done | bytes 2097168 | tf_op jit(solution)/shard_map/reduce_scatter | solution.py:29
  201.7 0.0 reduce-scatter.8.cloned.1.call-start
  201.8 39.5 %reduce-scatter.6.cloned.1.call-done = f32[512,512]{1,0:T(8,128)} async-done(((f32[1024,512]{1,0:T(8,128)}), f32[512,512]{1,0:T(8,128)}) %reduce-scatter.6.cloned.1.call-update) | async-done | bytes 1048592 | tf_op jit(solution)/shard_map/reduce_scatter | solution.py:30
  241.2 0.0 reduce-scatter.8.cloned.1.call-update
  241.2 27.0 %reduce-scatter.8.cloned.1.call-done = f32[128,512]{1,0:T(8,128)} async-done(((f32[512,512]{1,0:T(8,128)}), f32[128,512]{1,0:T(8,128)}) %reduce-scatter.8.cloned.1.call-update) | async-done | bytes 262160 | tf_op jit(solution)/shard_map/reduce_scatter | solution.py:31
  268.3 1.9 fusion.6
  270.2 2.2 collective-permute-start
  272.4 1.2 collective-permute-done
  273.6 1.2 collective-permute-start.1
  274.8 6.4 %collective-permute-done.1 = f32[128,512]{1,0:T(8,128)S(1)} collective-permute-done((f32[128,512]{1,0:T(8,128)S(1)}, f32[128,512]{1,0:T(8,128)S(1)}, u32[]{:S(2)}, u32[]{:S(2)}) %collective-permute-start.1) | collective-permute-done | bytes 262176 | tf_op jit(solution)/shard_map/ppermute | solution.py:41
  281.2 0.8 multiply_subtract_fusion
  282.0 0.5 stack.2
  282.5 104.7 %all_to_all.5 = bf16[64,128,256]{2,1,0:T(8,128)(2,1)} all-to-all(bf16[64,128,256]{2,1,0:T(8,128)(2,1)S(1)} %stack.2), channel_id=1, replica_groups=mesh['island'=4,'xh'=2,'z'=8,'y'=4] {'xh','z','y'}, dimensions={0} | all-to-all | bytes 8388608 | tf_op jit(solution)/shard_map/all_to_all | solution.py:50
  387.2 3.9 collective-permute-start.2
  391.1 4.9 %fusion = bf16[256,256]{1,0:T(8,128)(2,1)S(1)} fusion(bf16[8192,256]{1,0:T(8,128)(2,1)} %bitcast.6, bf16[256,8192]{1,0:T(8,128)(2,1)} %param.7), kind=kOutput, calls=%fused_computation.2 | convolution fusion | flops 1073872896 | bytes 8519680 | tf_op jit(solution)/shard_map/dot_general | solution.py:53
  396.0 2.2 collective-permute-done.2
  398.2 3.5 select_bitcast_fusion.1
  401.7 0.8 copy.16
  (20 shorter events, 0.1 us)
Async XLA Ops:
  7.2 8.9 %copy-start = (bf16[256,512]{1,0:T(8,128)(2,1)S(1)}, bf16[256,512]{1,0:T(8,128)(2,1)}, u32[]{:S(2)}) copy-start(bf16[256,512]{1,0:T(8,128)(2,1)} %param.8) | copy-start | bytes 786436
  7.2 194.5 %reduce-scatter.4.cloned.1.call-start = ((), (), s32[]{:S(2)}) async-start(), calls=%async_computation.4 | async-start | bytes 18874368 | tf_op jit(solution)/shard_map/reduce_scatter | solution.py:29
  24.2 244.1 %copy-start.2 = (f32[128,512]{1,0:T(8,128)S(1)}, f32[128,512]{1,0:T(8,128)}, u32[]{:S(2)}) copy-start(f32[128,512]{1,0:T(8,128)} %param.9) | copy-start | bytes 786436
  24.2 244.1 %copy-start.5 = (f32[1,128,512]{2,1,0:T(8,128)S(1)}, f32[1,128,512]{2,1,0:T(8,128)}, u32[]{:S(2)}) copy-start(f32[1,128,512]{2,1,0:T(8,128)} %param.13) | copy-start | bytes 786436
  24.2 244.1 %copy-start.6 = (f32[1,128,512]{2,1,0:T(8,128)S(1)}, f32[1,128,512]{2,1,0:T(8,128)}, u32[]{:S(2)}) copy-start(f32[1,128,512]{2,1,0:T(8,128)} %param.12) | copy-start | bytes 786436
  24.2 244.1 %copy-start.7 = (f32[1,128,512]{2,1,0:T(8,128)S(1)}, f32[1,128,512]{2,1,0:T(8,128)}, u32[]{:S(2)}) copy-start(f32[1,128,512]{2,1,0:T(8,128)} %param.11) | copy-start | bytes 786436
  24.2 257.0 %copy-start.4 = (f32[128,512]{1,0:T(8,128)S(1)}, f32[128,512]{1,0:T(8,128)}, u32[]{:S(2)}) copy-start(f32[128,512]{1,0:T(8,128)} %param.10) | copy-start | bytes 786436
  24.2 217.0 %reduce-scatter.6.cloned.1.call-start = ((), (), s32[]{:S(2)}) async-start(), calls=%async_computation.5 | async-start | bytes 3145728 | tf_op jit(solution)/shard_map/reduce_scatter | solution.py:30
  201.7 66.6 %reduce-scatter.8.cloned.1.call-start = ((), (), s32[]{:S(2)}) async-start(), calls=%async_computation.6 | async-start | bytes 1310720 | tf_op jit(solution)/shard_map/reduce_scatter | solution.py:31
  270.2 3.4 collective-permute-start
  273.6 7.6 %collective-permute-start.1 = (f32[128,512]{1,0:T(8,128)S(1)}, f32[128,512]{1,0:T(8,128)S(1)}, u32[]{:S(2)}, u32[]{:S(2)}) collective-permute-start(f32[128,512]{1,0:T(8,128)S(1)} %add.50), channel_id=1, source_target_pairs={{0,128},{64,192},{128,0},{192,64},{1,129},{65,193},{129,1},{193,65... | collective-permute-start | bytes 786440 | tf_op jit(solution)/shard_map/ppermute | solution.py:41
  282.0 105.2 %copy-start.3 = (f32[128,512]{1,0:T(8,128)}, f32[128,512]{1,0:T(8,128)S(1)}, u32[]{:S(2)}) copy-start(f32[128,512]{1,0:T(8,128)S(1)} %get-tuple-element.20) | copy-start | bytes 786436
  387.2 11.0 %collective-permute-start.2 = (bf16[8192,256]{1,0:T(8,128)(2,1)}, bf16[8192,256]{1,0:T(8,128)(2,1)}, u32[]{:S(2)}, u32[]{:S(2)}) collective-permute-start(bf16[8192,256]{1,0:T(8,128)(2,1)} %bitcast.6), channel_id=1, source_target_pairs={{0,64},{64,0},{128,192},{192,128},{1,65},{65,1},{129,193},{193,129... | collective-permute-start | bytes 12582920 | tf_op jit(solution)/shard_map/ppermute | solution.py:52
  391.1 7.1 %copy-start.1 = (bf16[256,8192]{1,0:T(8,128)(2,1)S(1)}, bf16[256,8192]{1,0:T(8,128)(2,1)}, u32[]{:S(2)}) copy-start(bf16[256,8192]{1,0:T(8,128)(2,1)} %param.7) | copy-start | bytes 12582916
Sparse Core Ops, SparseCore 0:
  24.4 177.2 reduce-scatter.3
  204.2 36.9 reduce-scatter.5
  243.8 24.4 reduce-scatter.7
